TPU v7x, 512 devices: a whole 4x8x8 slice. The times are simulated.
512 devices in a mesh: ep: 128 (over y, z, core), dp: 4 (over x).
Axes of the slice: x: 4, y: 8, z: 8, core: 2. Of those that a mesh axis runs over, the one named last changes fastest.
Arguments:
- tokens: bfloat16 [2, 2048, 3584], P(None, ('ep', 'dp')), may hold values from -6 to 6
- routing: int32 [2, 2048, 8], P(None, 'ep'), may hold values from 0 to 127, all different within a row; in each aligned block of 16 rows (0 to 15, 16 to 31, ..., all dimensions but the last counted through in order) at most 2 rows name the same one
- gate_values: float32 [2, 2048, 8], P(None, 'ep'), may hold values from 0.05 to 0.5
- held_weight: bfloat16 [128, 3584, 1024], P('ep', None, 'dp'), may hold values from -0.09375 to 0.09375
- scale_table: float32 [128, 28, 8], P(None, None, 'dp'), may hold values from 0.25 to 4
- old_expert: int32 [128], replicated, may hold values from 0 to 127, as said below
- new_expert: int32 [128], replicated, may hold values from 0 to 127, as said below
Outputs:
- combined: bfloat16 [2, 2048, 1024], P(None, 'ep', 'dp')
- moved_weight: bfloat16 [128, 3584, 1024], P('ep', None, 'dp')
Inputs may be any that keep to these rules, and one draw needn't show every extreme that they name: `routing`: each row names 8 different experts; in each aligned block of 16 token rows of a step no expert is named by more than 2 rows. `old_expert`: A permutation of the experts over the slots. `new_expert`: A permutation of the experts over the slots; it equals old_expert except at exactly 32 slots, whose experts are permuted among themselves so that each of them changes.
All inputs are finite; a program needn't handle non-finite values.
Results may differ from a plain program's by a relative error of at most 0.0039.
Values may be sent and summed in bfloat16 or wider, within the bound.
No kernel may reach another device: no remote copies, remote signals or barrier semaphores. Data moves between devices by JAX's collectives and lax.ppermute only.
A program may use at most 64 MiB of HBM per device.

v0:
```python
import jax
import jax.numpy as jnp
from jax import lax
from jax.sharding import PartitionSpec as P


def inverse_place(expert_at):
    count = expert_at.shape[0]
    labels = jnp.arange(count, dtype=jnp.int32)
    match = expert_at[None, :] == labels[:, None]
    return jnp.sum(jnp.where(match, labels[None, :], 0), axis=1)


def source_slots(old_expert, new_expert):
    labels = jnp.arange(old_expert.shape[0], dtype=jnp.int32)
    match = old_expert[None, :] == new_expert[:, None]
    return jnp.sum(jnp.where(match, labels[None, :], 0), axis=1)


def route_targets(routing, owners, peers, capacity):
    steps, group_size, top_count = routing.shape
    labels = jnp.arange(peers, dtype=jnp.int32)
    pair_ids = routing.reshape(steps, group_size * top_count)
    onehot = (pair_ids[:, :, None] == labels[None, None, :]).astype(jnp.int32)
    before = jnp.cumsum(onehot, axis=1) - onehot
    rank = jnp.sum(before * onehot, axis=2)
    slot = owners[pair_ids]
    step = jnp.arange(steps, dtype=jnp.int32)[:, None]
    return (slot * steps + step) * capacity + rank


def shards(tokens, routing, gate_values, held_weight, scale_table, old_expert, new_expert):
    peers = lax.axis_size("ep")
    n_dp = lax.axis_size("dp")
    my_slot = lax.axis_index("ep")
    my_dp = lax.axis_index("dp")
    steps, group_size, top_count = routing.shape
    capacity = 2
    old_block = held_weight[0]
    rows, cols = old_block.shape
    row_part = rows // n_dp
    blk = rows // scale_table.shape[1]
    owners = inverse_place(old_expert)
    sources = source_slots(old_expert, new_expert)
    w_rows = lax.all_to_all(old_block, "dp", split_axis=0, concat_axis=1, tiled=True)
    my_scales = lax.all_gather(scale_table[old_expert[my_slot]], "dp", axis=1, tiled=True)
    row_blocks = row_part // blk
    my_scales = lax.dynamic_slice_in_dim(my_scales, my_dp * row_blocks, row_blocks, axis=0)
    widened = jnp.repeat(jnp.repeat(my_scales, blk, axis=0), blk, axis=1)
    w32 = w_rows.astype(jnp.float32) * widened
    w_hi = w32.astype(jnp.bfloat16)
    w_lo = (w32 - w_hi.astype(jnp.float32)).astype(jnp.bfloat16)
    feats = lax.all_to_all(tokens, "dp", split_axis=2, concat_axis=1, tiled=True)
    target = route_targets(routing, owners, peers, capacity)
    token_of = jnp.broadcast_to(
        jnp.arange(group_size, dtype=jnp.int32)[None, :, None], (steps, group_size, top_count)
    ).reshape(steps, -1)
    step_of = jnp.broadcast_to(jnp.arange(steps, dtype=jnp.int32)[:, None], token_of.shape)
    pick = (
        jnp.zeros((peers * steps * capacity,), jnp.int32)
        .at[target.reshape(-1)]
        .set((step_of * group_size + token_of).reshape(-1))
    )
    send_tokens = feats.reshape(steps * group_size, row_part)[pick]
    send_tokens = send_tokens.reshape(peers, steps * capacity * row_part)
    pieces = old_block.reshape(peers, rows // peers * cols)
    first = lax.all_to_all(
        jnp.concatenate([pieces, send_tokens], axis=1),
        "ep",
        split_axis=0,
        concat_axis=0,
        tiled=True,
    )
    piece_len = pieces.shape[1]
    gathered_pieces = jnp.take(first[:, :piece_len], sources, axis=0)
    arrived = first[:, piece_len:].reshape(peers * steps * capacity, row_part)
    partial = jnp.dot(arrived, w_hi, preferred_element_type=jnp.float32) + jnp.dot(
        arrived, w_lo, preferred_element_type=jnp.float32
    )
    hidden = lax.psum_scatter(partial, "dp", scatter_dimension=1, tiled=True)
    act = jax.nn.silu(hidden).astype(jnp.bfloat16)
    act = act.reshape(peers, steps * capacity * act.shape[1])
    second = lax.all_to_all(
        jnp.concatenate([gathered_pieces, act], axis=1),
        "ep",
        split_axis=0,
        concat_axis=0,
        tiled=True,
    )
    new_block = second[:, :piece_len].reshape(rows, cols)
    returned = second[:, piece_len:].reshape(peers * steps * capacity, -1)
    picked = returned[target].astype(jnp.float32).reshape(steps, group_size, top_count, -1)
    combined = jnp.sum(gate_values[:, :, :, None] * picked, axis=2).astype(jnp.bfloat16)
    return (combined, new_block[None])


def solution(mesh):
    placed = (
        P(None, ("ep", "dp"), None),
        P(None, "ep", None),
        P(None, "ep", None),
        P("ep", None, "dp"),
        P(None, None, "dp"),
        P(),
        P(),
    )
    return jax.shard_map(
        shards,
        mesh=mesh,
        in_specs=placed,
        out_specs=(P(None, "ep", "dp"), P("ep", None, "dp")),
        check_vma=False,
    )
```

profile of v0, /device:TPU:1, one launch (start us, length us, event | category | flops | bytes accessed | tf_op | source)
XLA Modules:
  0.0 288.5 jit_solution(11411212066454031922)
XLA Ops:
  7.2 3.8 %copy.43 = bf16[2,4,3584]{1,0,2:T(2,128)(2,1)S(1)} copy(bf16[2,4,3584]{2,1,0:T(4,128)(2,1)} %param.7) | data formatting | bytes 114688 | tf_op args[0]
  11.0 4.3 %reshape.277 = bf16[4,2,3584]{2,1,0:T(2,128)(2,1)} reshape(bf16[3584,2,4]{2,1,0:T(2,128)(2,1)S(1)} %bitcast.65) | data formatting | bytes 114688
  15.3 4.8 %all-to-all-start = ((bf16[4,2,3584]{2,1,0:T(2,128)(2,1)}), bf16[4,2,3584]{2,1,0:T(2,128)(2,1)S(1)}, u32[]{:S(2)}, u32[]{:S(2)}) async-start(bf16[4,2,3584]{2,1,0:T(2,128)(2,1)} %reshape.277), calls=%async_computation | async-start | bytes 114688 | tf_op jit(solution)/shard_map/all_to_all | solution.py:53
  21.1 1.9 gather_fusion
  24.6 4.5 %reshape_squeeze.3 = bf16[128,7168]{1,0:T(8,128)(2,1)} reshape(bf16[1,3584,256]{2,1,0:T(8,128)(2,1)} %param.10) | data formatting | bytes 3670016 | tf_op jit(solution)/shard_map/reshape;squeeze | solution.py:66
  29.0 4.6 %all-to-all-start.2 = ((bf16[4,896,256]{2,1,0:T(8,128)(2,1)}), bf16[4,896,256]{2,1,0:T(8,128)(2,1)}, u32[]{:S(2)}, u32[]{:S(2)}) async-start(bf16[4,896,256]{2,1,0:T(8,128)(2,1)} %bitcast.10), calls=%async_computation.2 | async-start | bytes 3670016 | tf_op jit(solution)/shard_map/all_to_all | solution.py:45
  33.6 3.9 %reshape.278 = bf16[3584,2,4]{2,1,0:T(2,128)(2,1)S(1)} reshape(bf16[4,2,3584]{2,1,0:T(2,128)(2,1)S(1)} %all-to-all-done) | data formatting | bytes 114688
  38.9 2.1 gather_fusion.1
  42.5 2.0 maximum_bitcast_fusion
  44.9 3.4 %reduce = bf16[128,10752]{1,0:T(8,128)(2,1)} reduce(bf16[128,1,10752]{2,0,1:T(8,128)(2,1)S(1)} %maximum_bitcast_fusion, bf16[]{:T(256)} %broadcast.167), dimensions={1}, to_apply=%copy.47.reduce_sub_computation | reduce | bytes 5505026 | tf_op jit(solution)/shard_map/all_to_all | solution.py:67
  48.4 4.2 %reshape.279 = bf16[128,2,5376]{2,1,0:T(2,128)(2,1)} reshape(bf16[128,10752]{1,0:T(8,128)(2,1)} %reduce) | data formatting | bytes 5505024
  52.6 22.5 %all-to-all-start.1 = ((bf16[128,2,5376]{2,1,0:T(2,128)(2,1)}), bf16[128,2,5376]{2,1,0:T(2,128)(2,1)S(1)}, u32[]{:S(2)}, u32[]{:S(2)}) async-start(bf16[128,2,5376]{2,1,0:T(2,128)(2,1)} %reshape.279), calls=%async_computation.1 | async-start | bytes 5505024 | tf_op jit(solution)/shard_map/all_to_all | solution.py:67
  77.9 6.9 %all-gather = f32[1,28,8]{1,0,2:T(1,128)S(1)} all-gather(f32[1,28,2]{1,0,2:T(1,128)S(1)} %copy.54), channel_id=2, replica_groups=mesh['ep'=128,'dp'=4] {'dp'}, dimensions={2}, use_global_device_ids=true | all-gather | bytes 1120 | tf_op jit(solution)/shard_map/all_gather | solution.py:46
  85.0 3.6 %convert_bitcast_fusion = f32[896,4,256]{2,0,1:T(8,128)} fusion(bf16[4,896,256]{2,1,0:T(8,128)(2,1)} %all-to-all-done.2), kind=kLoop, calls=%fused_computation.5 | loop fusion | flops 917504 | bytes 5505024 | tf_op jit(solution)/shard_map/convert_element_type | solution.py:50
  88.7 4.6 %copy.48 = f32[896,4,256]{0,2,1:T(8,128)} copy(f32[896,4,256]{2,0,1:T(8,128)} %convert_bitcast_fusion) | data formatting | bytes 7340032 | tf_op jit(solution)/shard_map/convert_element_type | solution.py:50
  93.3 4.5 %subtract_convert_fusion = (bf16[896,8,128]{0,2,1:T(8,128)(2,1)}, bf16[896,8,128]{0,2,1:T(8,128)(2,1)}) fusion(f32[896,8,128]{0,2,1:T(8,128)} %bitcast.59, f32[896,8]{0,1:T(8,128)S(1)} %broadcast_bitcast_fusion), kind=kLoop, calls=%fused_computation.6 | loop fusion | flops 4587520 | bytes 7368704 | tf_op jit(solution)/shard_map/convert_element_type | solution.py:52
  97.8 42.8 %all-to-all-done.1 = bf16[128,2,5376]{2,1,0:T(2,128)(2,1)S(1)} async-done(((bf16[128,2,5376]{2,1,0:T(2,128)(2,1)}), bf16[128,2,5376]{2,1,0:T(2,128)(2,1)S(1)}, u32[]{:S(2)}, u32[]{:S(2)}) %all-to-all-start.1) | async-done | bytes 2752544 | tf_op jit(solution)/shard_map/all_to_all | solution.py:67
  140.6 7.1 %reshape.280 = bf16[128,1,10752]{2,1,0:T(2,128)(2,1)} reshape(bf16[128,2,5376]{2,1,0:T(2,128)(2,1)S(1)} %all-to-all-done.1) | data formatting | bytes 5505024
  147.7 2.9 %copy.58 = bf16[128,1,10752]{2,0,1:T(8,128)(2,1)S(1)} copy(bf16[128,1,10752]{2,1,0:T(2,128)(2,1)} %reshape.280) | data formatting | bytes 5505024
  153.8 2.6 fusion.10
  156.4 2.6 convolution_add_fusion
  160.7 2.9 %gather_fusion.2 = bf16[128,7168]{1,0:T(8,128)(2,1)} fusion(bf16[128,7168]{1,0:T(8,128)(2,1)S(1)} %slice.24, s32[1024]{0:T(1024)S(1)} %pad_clamp_fusion.1), kind=kCustom, calls=%fused_computation.2 | custom fusion | bytes 3670528 | tf_op jit(solution)/shard_map/jit(_take)/gather | solution.py:75
  163.6 3.0 %broadcast_select_fusion = bf16[128,7168]{1,0:T(8,128)(2,1)} fusion(bf16[128,7168]{1,0:T(8,128)(2,1)} %gather_fusion.2, pred[128]{0:T(512)(128)(4,1)S(1)} %compare_and_fusion), kind=kLoop, calls=%fused_computation.12 | loop fusion | flops 917504 | bytes 3670144 | tf_op jit(solution)/shard_map/jit(_take)/select_n | solution.py:75
  166.6 21.2 %reduce-scatter.2.cloned.1.call-done = f32[512,256]{1,0:T(8,128)} async-done(((f32[512,1024]{1,0:T(8,128)}), f32[512,256]{1,0:T(8,128)}) %reduce-scatter.2.cloned.1.call-update) | async-done | bytes 524304 | tf_op jit(solution)/shard_map/reduce_scatter | solution.py:80
  189.1 1.6 maximum_bitcast_fusion.1
  190.7 2.9 %reduce.1 = bf16[128,8192]{1,0:T(8,128)(2,1)} reduce(bf16[128,1,8192]{2,0,1:T(8,128)(2,1)S(1)} %maximum_bitcast_fusion.1, bf16[]{:T(256)} %broadcast.167), dimensions={1}, to_apply=%copy.51.reduce_sub_computation | reduce | bytes 4194306 | tf_op jit(solution)/shard_map/all_to_all | solution.py:83
  193.7 4.5 %reshape.281 = bf16[128,2,4096]{2,1,0:T(2,128)(2,1)} reshape(bf16[128,8192]{1,0:T(8,128)(2,1)} %reduce.1) | data formatting | bytes 4194304
  198.2 14.5 %all-to-all-start.3 = ((bf16[128,2,4096]{2,1,0:T(2,128)(2,1)}), bf16[128,2,4096]{2,1,0:T(2,128)(2,1)S(1)}, u32[]{:S(2)}, u32[]{:S(2)}) async-start(bf16[128,2,4096]{2,1,0:T(2,128)(2,1)} %reshape.281), calls=%async_computation.4 | async-start | bytes 4194304 | tf_op jit(solution)/shard_map/all_to_all | solution.py:83
  212.8 52.0 %all-to-all-done.3 = bf16[128,2,4096]{2,1,0:T(2,128)(2,1)S(1)} async-done(((bf16[128,2,4096]{2,1,0:T(2,128)(2,1)}), bf16[128,2,4096]{2,1,0:T(2,128)(2,1)S(1)}, u32[]{:S(2)}, u32[]{:S(2)}) %all-to-all-start.3) | async-done | bytes 2097184 | tf_op jit(solution)/shard_map/all_to_all | solution.py:83
  264.8 6.8 %reshape.282 = bf16[128,1,8192]{2,1,0:T(2,128)(2,1)} reshape(bf16[128,2,4096]{2,1,0:T(2,128)(2,1)S(1)} %all-to-all-done.3) | data formatting | bytes 4194304
  271.6 4.5 %copy.59 = bf16[128,1,8192]{2,0,1:T(8,128)(2,1)S(1)} copy(bf16[128,1,8192]{2,1,0:T(2,128)(2,1)} %reshape.282) | data formatting | bytes 4194304
  276.4 3.3 %broadcast_in_dim_reshape.4 = bf16[1,3584,256]{2,1,0:T(8,128)(2,1)} reshape(bf16[128,7168]{1,0:T(8,128)(2,1)S(1)} %slice.27) | data formatting | bytes 3670016 | tf_op jit(solution)/shard_map/broadcast_in_dim;reshape | solution.py:94
  (68 shorter events, 15.3 us)
Async XLA Ops:
  7.2 70.5 %copy-start = (f32[128,28,2]{0,2,1:T(2,128)S(1)}, f32[128,28,2]{0,2,1:T(2,128)}, u32[]{:S(2)}) copy-start(f32[128,28,2]{0,2,1:T(2,128)} %param.11) | copy-start | bytes 86020
  7.2 12.9 %copy-start.6 = (s32[2,16,8]{1,2,0:T(8,128)S(1)}, s32[2,16,8]{1,2,0:T(8,128)}, u32[]{:S(2)}) copy-start(s32[2,16,8]{1,2,0:T(8,128)} %param.8) | copy-start | bytes 3076
  7.2 13.7 %copy-start.9 = (s32[128]{0:T(128)S(1)}, s32[128]{0:T(128)}, u32[]{:S(2)}) copy-start(s32[128]{0:T(128)} %param.12) | copy-start | bytes 1540
  7.2 13.7 %copy-start.8 = (s32[128]{0:T(128)S(1)}, s32[128]{0:T(128)}, u32[]{:S(2)}) copy-start(s32[128]{0:T(128)} %param.13) | copy-start | bytes 1540
  15.3 13.8 %all-to-all-start = ((bf16[4,2,3584]{2,1,0:T(2,128)(2,1)}), bf16[4,2,3584]{2,1,0:T(2,128)(2,1)S(1)}, u32[]{:S(2)}, u32[]{:S(2)}) async-start(bf16[4,2,3584]{2,1,0:T(2,128)(2,1)} %reshape.277), calls=%async_computation | async-start | bytes 114688 | tf_op jit(solution)/shard_map/all_to_all | solution.py:53
  29.0 23.6 %all-to-all-start.2 = ((bf16[4,896,256]{2,1,0:T(8,128)(2,1)}), bf16[4,896,256]{2,1,0:T(8,128)(2,1)}, u32[]{:S(2)}, u32[]{:S(2)}) async-start(bf16[4,896,256]{2,1,0:T(8,128)(2,1)} %bitcast.10), calls=%async_computation.2 | async-start | bytes 3670016 | tf_op jit(solution)/shard_map/all_to_all | solution.py:45
  52.6 88.0 %all-to-all-start.1 = ((bf16[128,2,5376]{2,1,0:T(2,128)(2,1)}), bf16[128,2,5376]{2,1,0:T(2,128)(2,1)S(1)}, u32[]{:S(2)}, u32[]{:S(2)}) async-start(bf16[128,2,5376]{2,1,0:T(2,128)(2,1)} %reshape.279), calls=%async_computation.1 | async-start | bytes 5505024 | tf_op jit(solution)/shard_map/all_to_all | solution.py:67
  75.1 112.7 %reduce-scatter.2.cloned.1.call-start = ((), (), s32[]{:S(2)}) async-start(), calls=%async_computation.5 | async-start | bytes 2621440 | tf_op jit(solution)/shard_map/reduce_scatter | solution.py:80
  150.6 1.6 copy-start.2
  150.6 3.1 %copy-start.4 = (bf16[896,8,128]{0,2,1:T(8,128)(2,1)S(1)}, bf16[896,8,128]{0,2,1:T(8,128)(2,1)}, u32[]{:S(2)}) copy-start(bf16[896,8,128]{0,2,1:T(8,128)(2,1)} %get-tuple-element.5) | copy-start | bytes 5505028
  153.8 2.6 copy-start.3
  153.8 2.6 copy-start.5
  198.2 14.5 %copy-start.7 = (f32[2,16,8]{1,2,0:T(8,128)S(1)}, f32[2,16,8]{1,2,0:T(8,128)}, u32[]{:S(2)}) copy-start(f32[2,16,8]{1,2,0:T(8,128)} %param.9) | copy-start | bytes 3076
  198.2 66.6 %all-to-all-start.3 = ((bf16[128,2,4096]{2,1,0:T(2,128)(2,1)}), bf16[128,2,4096]{2,1,0:T(2,128)(2,1)S(1)}, u32[]{:S(2)}, u32[]{:S(2)}) async-start(bf16[128,2,4096]{2,1,0:T(2,128)(2,1)} %reshape.281), calls=%async_computation.4 | async-start | bytes 4194304 | tf_op jit(solution)/shard_map/all_to_all | solution.py:83
  276.2 5.4 %copy-start.1 = (f32[128,28,2]{0,2,1:T(2,128)S(1)}, f32[128,28,2]{0,2,1:T(2,128)}, u32[]{:S(2)}) copy-start(f32[128,28,2]{0,2,1:T(2,128)} %param.11) | copy-start | bytes 86020
Sparse Core Ops, SparseCore 0:
  159.1 28.5 reduce-scatter.1
where the time goes:
time: 290 us; the launch traced here: 288 us
  waiting for transfers between devices  116 us (40%)
  local copies, waits for them, and re-layouts  73.7 us (25%)
  starting transfers between devices  46.4 us (16%)
  other arithmetic  23.8 us (8%)
  between operations  16.3 us (6%)
  blocking collectives  6.95 us (2%)
  matrix products  5.21 us (2%)
    all_to_all x1, waiting for transfers between devices, shards(): lax.all_to_all(jnp.concatenate([gathered_pieces, act], axis=1), 'ep', spl...  52 us
    unnamed x33, local copies, waits for them, and re-layouts  43.8 us
    all_to_all x1, waiting for transfers between devices, shards(): lax.all_to_all(jnp.concatenate([pieces, send_tokens], axis=1), 'ep', spli...  42.8 us
    all_to_all x1, starting transfers between devices, shards(): lax.all_to_all(jnp.concatenate([pieces, send_tokens], axis=1), 'ep', spli...  22.5 us
    reduce_scatter x1, waiting for transfers between devices, shards(): hidden = lax.psum_scatter(partial, 'dp', scatter_dimension=1, tiled=True)  21.2 us
    all_to_all x1, starting transfers between devices, shards(): lax.all_to_all(jnp.concatenate([gathered_pieces, act], axis=1), 'ep', spl...  14.5 us
    all_gather x1, blocking collectives, shards(): lax.all_gather(scale_table[old_expert[my_slot]], 'dp', axis=1, tiled=True)  6.95 us
  transfers between devices with their start and end apart: 5, of which 3 were waited for; matrix products, arithmetic and copies ran while one was open for 17% of the time, Pallas kernels for 0%

commit v1 on v0

--- a/solution.py
+++ b/solution.py
@@ -43,7 +43,12 @@
     owners = inverse_place(old_expert)
     sources = source_slots(old_expert, new_expert)
     w_rows = lax.all_to_all(old_block, "dp", split_axis=0, concat_axis=1, tiled=True)
-    my_scales = lax.all_gather(scale_table[old_expert[my_slot]], "dp", axis=1, tiled=True)
+    my_scales = jnp.concatenate(
+        lax.all_to_all(
+            jnp.stack([scale_table[old_expert[my_slot]]] * lax.axis_size("dp")), "dp", 0, 0
+        ),
+        axis=1,
+    )
     row_blocks = row_part // blk
     my_scales = lax.dynamic_slice_in_dim(my_scales, my_dp * row_blocks, row_blocks, axis=0)
     widened = jnp.repeat(jnp.repeat(my_scales, blk, axis=0), blk, axis=1)

time: 290 us -> 299 us (1.031)
  waiting for transfers between devices: 116 us -> 125 us
  blocking collectives: 6.95 us -> 0 us
  starting transfers between devices: 46.4 us -> 50.9 us
    all_to_all x1, waiting for transfers between devices: 42.8 us -> 52.3 us  [shards(): lax.all_to_all(jnp.concatenate([pieces, send_tokens], axis=1), 'ep', spli...]
    all_gather x1 -> x0, blocking collectives: 6.95 us -> none  [shards(): lax.all_gather(scale_table[old_expert[my_slot]], 'dp', axis=1, tiled=True)]
    all_to_all x0 -> x1, starting transfers between devices: none -> 4.83 us  [shards(): lax.all_to_all(jnp.stack([scale_table[old_expert[my_slot]]] * lax.axis_si...]
    unnamed x33 -> x25, local copies, waits for them, and re-layouts: 43.8 us -> 44.3 us
  transfers between devices with their start and end apart: 5 -> 6, of which waited for: 3 -> 3; matrix products, arithmetic and copies ran while one was open for 17% -> 19% of each run, Pallas kernels for 0% -> 0%
where the time goes in v1:
time: 299 us; the launch traced here: 298 us
  waiting for transfers between devices  125 us (42%)
  local copies, waits for them, and re-layouts  75.6 us (25%)
  starting transfers between devices  50.9 us (17%)
  other arithmetic  24.5 us (8%)
  between operations  16.3 us (5%)
  matrix products  5.22 us (2%)
    all_to_all x1, waiting for transfers between devices, shards(): lax.all_to_all(jnp.concatenate([pieces, send_tokens], axis=1), 'ep', spli...  52.3 us
    all_to_all x1, waiting for transfers between devices, shards(): lax.all_to_all(jnp.concatenate([gathered_pieces, act], axis=1), 'ep', spl...  52 us
    unnamed x25, local copies, waits for them, and re-layouts  44.3 us
    all_to_all x1, starting transfers between devices, shards(): lax.all_to_all(jnp.concatenate([pieces, send_tokens], axis=1), 'ep', spli...  22.5 us
    reduce_scatter x1, waiting for transfers between devices, shards(): hidden = lax.psum_scatter(partial, 'dp', scatter_dimension=1, tiled=True)  21.2 us
    all_to_all x1, starting transfers between devices, shards(): lax.all_to_all(jnp.concatenate([gathered_pieces, act], axis=1), 'ep', spl...  14.5 us
  transfers between devices with their start and end apart: 6, of which 3 were waited for; matrix products, arithmetic and copies ran while one was open for 19% of the time, Pallas kernels for 0%

profile of v1, /device:TPU:1, one launch (start us, length us, event | category | flops | bytes accessed | tf_op | source)
XLA Modules:
  0.0 298.0 jit_solution(16808319060570230638)
XLA Ops:
  11.2 4.8 %all-to-all-start.3 = ((f32[4,28,2]{1,2,0:T(2,128)}), f32[4,28,2]{1,2,0:T(2,128)S(1)}, u32[]{:S(2)}, u32[]{:S(2)}) async-start(f32[4,28,2]{1,2,0:T(2,128)} %stack.3), calls=%async_computation.3 | async-start | bytes 8192 | tf_op jit(solution)/shard_map/all_to_all | solution.py:47
  18.4 1.9 gather_fusion
  20.4 3.7 %copy.46 = bf16[2,4,3584]{1,0,2:T(2,128)(2,1)S(1)} copy(bf16[2,4,3584]{2,1,0:T(4,128)(2,1)} %param.7) | data formatting | bytes 114688 | tf_op args[0]
  24.2 4.3 %reshape.284 = bf16[4,2,3584]{2,1,0:T(2,128)(2,1)} reshape(bf16[3584,2,4]{2,1,0:T(2,128)(2,1)S(1)} %bitcast.68) | data formatting | bytes 114688
  29.8 4.2 %all-to-all-start = ((bf16[4,2,3584]{2,1,0:T(2,128)(2,1)}), bf16[4,2,3584]{2,1,0:T(2,128)(2,1)S(1)}, u32[]{:S(2)}, u32[]{:S(2)}) async-start(bf16[4,2,3584]{2,1,0:T(2,128)(2,1)} %reshape.284), calls=%async_computation | async-start | bytes 114688 | tf_op jit(solution)/shard_map/all_to_all | solution.py:58
  34.1 4.5 %reshape_squeeze.3 = bf16[128,7168]{1,0:T(8,128)(2,1)} reshape(bf16[1,3584,256]{2,1,0:T(8,128)(2,1)} %param.10) | data formatting | bytes 3670016 | tf_op jit(solution)/shard_map/reshape;squeeze | solution.py:71
  38.6 4.6 %all-to-all-start.2 = ((bf16[4,896,256]{2,1,0:T(8,128)(2,1)}), bf16[4,896,256]{2,1,0:T(8,128)(2,1)}, u32[]{:S(2)}, u32[]{:S(2)}) async-start(bf16[4,896,256]{2,1,0:T(8,128)(2,1)} %bitcast.10), calls=%async_computation.2 | async-start | bytes 3670016 | tf_op jit(solution)/shard_map/all_to_all | solution.py:45
  43.2 3.9 %reshape.285 = bf16[3584,2,4]{2,1,0:T(2,128)(2,1)S(1)} reshape(bf16[4,2,3584]{2,1,0:T(2,128)(2,1)S(1)} %all-to-all-done) | data formatting | bytes 114688
  48.4 2.1 gather_fusion.1
  52.0 2.0 maximum_bitcast_fusion
  54.5 3.4 %reduce = bf16[128,10752]{1,0:T(8,128)(2,1)} reduce(bf16[128,1,10752]{2,0,1:T(8,128)(2,1)S(1)} %maximum_bitcast_fusion, bf16[]{:T(256)} %broadcast.168), dimensions={1}, to_apply=%copy.50.reduce_sub_computation | reduce | bytes 5505026 | tf_op jit(solution)/shard_map/all_to_all | solution.py:72
  57.9 4.2 %reshape.286 = bf16[128,2,5376]{2,1,0:T(2,128)(2,1)} reshape(bf16[128,10752]{1,0:T(8,128)(2,1)} %reduce) | data formatting | bytes 5505024
  62.1 22.5 %all-to-all-start.1 = ((bf16[128,2,5376]{2,1,0:T(2,128)(2,1)}), bf16[128,2,5376]{2,1,0:T(2,128)(2,1)S(1)}, u32[]{:S(2)}, u32[]{:S(2)}) async-start(bf16[128,2,5376]{2,1,0:T(2,128)(2,1)} %reshape.286), calls=%async_computation.1 | async-start | bytes 5505024 | tf_op jit(solution)/shard_map/all_to_all | solution.py:72
  85.1 3.6 %convert_bitcast_fusion = f32[896,4,256]{2,0,1:T(8,128)} fusion(bf16[4,896,256]{2,1,0:T(8,128)(2,1)} %all-to-all-done.2), kind=kLoop, calls=%fused_computation.5 | loop fusion | flops 917504 | bytes 5505024 | tf_op jit(solution)/shard_map/convert_element_type | solution.py:55
  88.7 4.6 %copy.51 = f32[896,4,256]{0,2,1:T(8,128)} copy(f32[896,4,256]{2,0,1:T(8,128)} %convert_bitcast_fusion) | data formatting | bytes 7340032 | tf_op jit(solution)/shard_map/convert_element_type | solution.py:55
  93.3 4.5 %subtract_convert_fusion = (bf16[896,8,128]{0,2,1:T(8,128)(2,1)}, bf16[896,8,128]{0,2,1:T(8,128)(2,1)}) fusion(f32[896,8,128]{0,2,1:T(8,128)} %bitcast.62, f32[896,8]{0,1:T(8,128)S(1)} %broadcast_bitcast_fusion), kind=kLoop, calls=%fused_computation.6 | loop fusion | flops 4587520 | bytes 7368704 | tf_op jit(solution)/shard_map/convert_element_type | solution.py:57
  97.9 52.3 %all-to-all-done.1 = bf16[128,2,5376]{2,1,0:T(2,128)(2,1)S(1)} async-done(((bf16[128,2,5376]{2,1,0:T(2,128)(2,1)}), bf16[128,2,5376]{2,1,0:T(2,128)(2,1)S(1)}, u32[]{:S(2)}, u32[]{:S(2)}) %all-to-all-start.1) | async-done | bytes 2752544 | tf_op jit(solution)/shard_map/all_to_all | solution.py:72
  150.1 7.1 %reshape.287 = bf16[128,1,10752]{2,1,0:T(2,128)(2,1)} reshape(bf16[128,2,5376]{2,1,0:T(2,128)(2,1)S(1)} %all-to-all-done.1) | data formatting | bytes 5505024
  157.2 2.9 copy.59
  163.3 2.6 fusion.10
  165.9 2.6 convolution_add_fusion
  170.2 2.9 gather_fusion.2
  173.1 3.0 broadcast_select_fusion
  176.1 21.2 %reduce-scatter.2.cloned.1.call-done = f32[512,256]{1,0:T(8,128)} async-done(((f32[512,1024]{1,0:T(8,128)}), f32[512,256]{1,0:T(8,128)}) %reduce-scatter.2.cloned.1.call-update) | async-done | bytes 524304 | tf_op jit(solution)/shard_map/reduce_scatter | solution.py:85
  198.6 1.6 maximum_bitcast_fusion.1
  200.3 2.9 reduce.1
  203.2 4.5 %reshape.288 = bf16[128,2,4096]{2,1,0:T(2,128)(2,1)} reshape(bf16[128,8192]{1,0:T(8,128)(2,1)} %reduce.1) | data formatting | bytes 4194304
  207.7 14.5 %all-to-all-start.4 = ((bf16[128,2,4096]{2,1,0:T(2,128)(2,1)}), bf16[128,2,4096]{2,1,0:T(2,128)(2,1)S(1)}, u32[]{:S(2)}, u32[]{:S(2)}) async-start(bf16[128,2,4096]{2,1,0:T(2,128)(2,1)} %reshape.288), calls=%async_computation.5 | async-start | bytes 4194304 | tf_op jit(solution)/shard_map/all_to_all | solution.py:88
  222.3 52.0 %all-to-all-done.4 = bf16[128,2,4096]{2,1,0:T(2,128)(2,1)S(1)} async-done(((bf16[128,2,4096]{2,1,0:T(2,128)(2,1)}), bf16[128,2,4096]{2,1,0:T(2,128)(2,1)S(1)}, u32[]{:S(2)}, u32[]{:S(2)}) %all-to-all-start.4) | async-done | bytes 2097184 | tf_op jit(solution)/shard_map/all_to_all | solution.py:88
  274.3 6.8 %reshape.289 = bf16[128,1,8192]{2,1,0:T(2,128)(2,1)} reshape(bf16[128,2,4096]{2,1,0:T(2,128)(2,1)S(1)} %all-to-all-done.4) | data formatting | bytes 4194304
  281.1 4.5 %copy.60 = bf16[128,1,8192]{2,0,1:T(8,128)(2,1)S(1)} copy(bf16[128,1,8192]{2,1,0:T(2,128)(2,1)} %reshape.289) | data formatting | bytes 4194304
  285.9 3.3 %broadcast_in_dim_reshape.4 = bf16[1,3584,256]{2,1,0:T(8,128)(2,1)} reshape(bf16[128,7168]{1,0:T(8,128)(2,1)S(1)} %slice.27) | data formatting | bytes 3670016 | tf_op jit(solution)/shard_map/broadcast_in_dim;reshape | solution.py:99
  (64 shorter events, 18.2 us)
Async XLA Ops:
  7.2 3.2 %copy-start = (f32[128,28,2]{0,2,1:T(2,128)S(1)}, f32[128,28,2]{0,2,1:T(2,128)}, u32[]{:S(2)}) copy-start(f32[128,28,2]{0,2,1:T(2,128)} %param.11) | copy-start | bytes 86020
  11.2 18.6 %all-to-all-start.3 = ((f32[4,28,2]{1,2,0:T(2,128)}), f32[4,28,2]{1,2,0:T(2,128)S(1)}, u32[]{:S(2)}, u32[]{:S(2)}) async-start(f32[4,28,2]{1,2,0:T(2,128)} %stack.3), calls=%async_computation.3 | async-start | bytes 8192 | tf_op jit(solution)/shard_map/all_to_all | solution.py:47
  29.8 8.7 %all-to-all-start = ((bf16[4,2,3584]{2,1,0:T(2,128)(2,1)}), bf16[4,2,3584]{2,1,0:T(2,128)(2,1)S(1)}, u32[]{:S(2)}, u32[]{:S(2)}) async-start(bf16[4,2,3584]{2,1,0:T(2,128)(2,1)} %reshape.284), calls=%async_computation | async-start | bytes 114688 | tf_op jit(solution)/shard_map/all_to_all | solution.py:58
  38.6 23.6 %all-to-all-start.2 = ((bf16[4,896,256]{2,1,0:T(8,128)(2,1)}), bf16[4,896,256]{2,1,0:T(8,128)(2,1)}, u32[]{:S(2)}, u32[]{:S(2)}) async-start(bf16[4,896,256]{2,1,0:T(8,128)(2,1)} %bitcast.10), calls=%async_computation.2 | async-start | bytes 3670016 | tf_op jit(solution)/shard_map/all_to_all | solution.py:45
  62.1 88.0 %all-to-all-start.1 = ((bf16[128,2,5376]{2,1,0:T(2,128)(2,1)}), bf16[128,2,5376]{2,1,0:T(2,128)(2,1)S(1)}, u32[]{:S(2)}, u32[]{:S(2)}) async-start(bf16[128,2,5376]{2,1,0:T(2,128)(2,1)} %reshape.286), calls=%async_computation.1 | async-start | bytes 5505024 | tf_op jit(solution)/shard_map/all_to_all | solution.py:72
  84.6 112.7 %reduce-scatter.2.cloned.1.call-start = ((), (), s32[]{:S(2)}) async-start(), calls=%async_computation.6 | async-start | bytes 2621440 | tf_op jit(solution)/shard_map/reduce_scatter | solution.py:85
  160.2 1.6 copy-start.2
  160.2 3.1 %copy-start.4 = (bf16[896,8,128]{0,2,1:T(8,128)(2,1)S(1)}, bf16[896,8,128]{0,2,1:T(8,128)(2,1)}, u32[]{:S(2)}) copy-start(bf16[896,8,128]{0,2,1:T(8,128)(2,1)} %get-tuple-element.5) | copy-start | bytes 5505028
  163.3 2.6 copy-start.3
  163.3 2.6 copy-start.5
  207.7 14.5 %copy-start.6 = (f32[2,16,8]{1,2,0:T(8,128)S(1)}, f32[2,16,8]{1,2,0:T(8,128)}, u32[]{:S(2)}) copy-start(f32[2,16,8]{1,2,0:T(8,128)} %param.9) | copy-start | bytes 3076
  207.7 66.6 %all-to-all-start.4 = ((bf16[128,2,4096]{2,1,0:T(2,128)(2,1)}), bf16[128,2,4096]{2,1,0:T(2,128)(2,1)S(1)}, u32[]{:S(2)}, u32[]{:S(2)}) async-start(bf16[128,2,4096]{2,1,0:T(2,128)(2,1)} %reshape.288), calls=%async_computation.5 | async-start | bytes 4194304 | tf_op jit(solution)/shard_map/all_to_all | solution.py:88
  285.8 5.4 %copy-start.1 = (f32[128,28,2]{0,2,1:T(2,128)S(1)}, f32[128,28,2]{0,2,1:T(2,128)}, u32[]{:S(2)}) copy-start(f32[128,28,2]{0,2,1:T(2,128)} %param.11) | copy-start | bytes 86020
Sparse Core Ops, SparseCore 0:
  168.7 28.5 reduce-scatter.1
